TPU v7x, 256 devices: a whole 4x4x8 slice. The times are simulated.
256 devices in a mesh: dp: 32 (over x_lo, z, core), tensor: 8 (over x_hi, y).
Axes of the slice: x: 4 (x_hi: 2, x_lo: 2; x = x_hi * 2 + x_lo), y: 4, z: 8, core: 2. Of those that a mesh axis runs over, the one named last changes fastest.
Arguments:
- hidden_input_state: bfloat16 [12288, 4608], P('dp', 'tensor'), may hold values from -80 to 80
- norm_gain: float32 [4608], replicated, may hold values from 0.5 to 1.5
- head_weight: bfloat16 [4608, 8192], P(None, 'tensor'), may hold values from -2 to 2
- target_ids: int32 [12288], P('dp'), may hold values from 0 to 8191
Outputs:
- hidden_state_gradient: float32 [12288, 4608], P('dp', 'tensor')
- grad_head: float32 [4608, 8192], P('dp', 'tensor')
- norm_gain_gradient: float32 [4608], P('tensor')
All inputs are finite; a program needn't handle non-finite values.
Results may differ from a plain program's by a relative error of at most 0.0039.
Values may be sent and summed in bfloat16 or wider, within the bound.
No kernel may reach another device: no remote copies, remote signals or barrier semaphores. Data moves between devices by JAX's collectives and lax.ppermute only.
A program may use at most 192 MiB of HBM per device.

v0:
```python
import jax
import jax.numpy as jnp
from jax import lax
from jax.sharding import PartitionSpec as P

epsilon = 1e-06


def shards(hidden_input_state, norm_gain, head_weight, target_ids):
    local_cols = hidden_input_state.shape[1]
    vocab_rows = head_weight.shape[1]
    width = head_weight.shape[0]
    gathered = lax.all_gather(hidden_input_state, "tensor", axis=1, tiled=True)
    values = gathered.astype(jnp.float32)
    scaled_rows = lax.rsqrt(jnp.mean(values * values, axis=1, keepdims=True) + epsilon)
    normed = (values * scaled_rows * norm_gain[None, :]).astype(jnp.bfloat16)
    logits = jnp.dot(normed, head_weight, preferred_element_type=jnp.float32)
    local_top = jnp.max(logits, axis=1)
    local_total = jnp.sum(jnp.exp(logits - local_top[:, None]), axis=1)
    row_top = lax.pmax(local_top, "tensor")
    row_total = lax.psum(local_total * jnp.exp(local_top - row_top), "tensor")
    log_total = row_top + jnp.log(row_total)
    offset = lax.axis_index("tensor") * vocab_rows
    column_ids = offset + lax.broadcasted_iota(jnp.int32, (1, vocab_rows), 1)
    onehot = (column_ids == target_ids[:, None]).astype(jnp.float32)
    dlogits = (jnp.exp(logits - log_total[:, None]) - onehot).astype(jnp.bfloat16)
    start_col = lax.axis_index("tensor") * local_cols
    normalized_slice = hidden_input_state.astype(jnp.float32) * scaled_rows
    gain_slice = lax.dynamic_slice_in_dim(norm_gain, start_col, local_cols)
    grad_cols = lax.psum_scatter(
        lax.dot_general(
            head_weight, dlogits, (((1,), (1,)), ((), ())), preferred_element_type=jnp.float32
        ),
        "tensor",
        scatter_dimension=0,
        tiled=True,
    )
    normed_gradient = grad_cols.T
    partial_inner_sum = jnp.sum(normed_gradient * gain_slice[None, :] * normalized_slice, axis=1)
    row_inner_sum = lax.psum(partial_inner_sum, "tensor") / width
    weighted_rows = normed_gradient * gain_slice[None, :]
    hidden_state_gradient = scaled_rows * (
        weighted_rows - normalized_slice * row_inner_sum[:, None]
    )
    norm_gain_gradient = lax.psum(jnp.sum(normed_gradient * normalized_slice, axis=0), "dp")
    grad_head = lax.psum_scatter(
        lax.dot_general(
            normed, dlogits, (((0,), (0,)), ((), ())), preferred_element_type=jnp.float32
        ),
        "dp",
        scatter_dimension=0,
        tiled=True,
    )
    return (hidden_state_gradient, grad_head, norm_gain_gradient)


def solution(mesh):
    return jax.shard_map(
        shards,
        mesh=mesh,
        in_specs=(P("dp", "tensor"), P(), P(None, "tensor"), P("dp")),
        out_specs=(P("dp", "tensor"), P("dp", "tensor"), P("tensor")),
        check_vma=False,
    )
```

profile of v0, /device:TPU:4, one launch (start us, length us, event | category | flops | bytes accessed | tf_op | source)
XLA Modules:
  0.0 423.8 jit_solution(17505398155015696289)
XLA Ops:
  7.2 0.0 all-gather.2.cloned.1.call-start
  7.2 0.7 all-gather.2.cloned.1.call-update
  7.9 0.0 reduce-scatter.7.cloned.1.call-start
  8.0 74.1 %all-gather.2.cloned.1.call-done = bf16[384,4608]{0,1:T(8,128)(2,1)} async-done(((bf16[384,576]{0,1:T(8,128)(2,1)}), bf16[384,4608]{0,1:T(8,128)(2,1)}) %all-gather.2.cloned.1.call-update) | async-done | bytes 3538960 | tf_op jit(solution)/shard_map/all_gather | solution.py:13
  82.1 0.0 copy-start
  82.1 3.0 fusion
  85.1 0.1 copy-done
  85.2 8.8 %fusion.8 = (f32[384]{0:T(512)S(1)}, f32[384,1024]{1,0:T(8,128)}) fusion(bf16[4608,1024]{1,0:T(8,128)(2,1)} %param.6, bf16[384,4608]{0,1:T(8,128)(2,1)S(1)} %copy-done, f32[4608]{0:T(1024)} %param.5, f32[384]{0:T(512)S(1)} %add_rsqrt_fusion), kind=kOutput, calls=%fused_computation.21 | convolution fusion | flops 3631349248 | bytes 14570496 | tf_op jit(solution)/shard_map/dot_general | solution.py:17
  93.9 22.2 %pmax.7 = f32[384]{0:T(512)S(1)} all-reduce(f32[384]{0:T(512)S(1)} %get-tuple-element.11), channel_id=1, replica_groups=mesh['dp'=32,'tensor'=8] {'tensor'}, use_global_device_ids=true, to_apply=%region_2.0 | all-reduce | flops 384 | bytes 3072 | tf_op jit(solution)/shard_map/pmax | solution.py:20
  116.1 1.8 exponential_reduce_fusion
  117.9 0.6 exponential_multiply_fusion
  118.5 19.1 %psum.21 = f32[384]{0:T(512)S(1)} all-reduce(f32[384]{0:T(512)} %exponential_multiply_fusion), channel_id=1, replica_groups=mesh['dp'=32,'tensor'=8] {'tensor'}, use_global_device_ids=true, to_apply=%region_4.0 | all-reduce | flops 384 | bytes 3072 | tf_op jit(solution)/shard_map/psum | solution.py:21
  137.6 0.0 copy-start.2
  137.6 0.6 copy-done.2
  138.2 11.1 %convolution_bitcast_fusion = f32[4608,384]{0,1:T(8,128)} fusion(bf16[4608,1024]{1,0:T(8,128)(2,1)} %param.6, f32[384,1024]{1,0:T(8,128)} %get-tuple-element.12, s32[1024]{0:T(1024)S(1)} %iota_add_fusion, f32[384]{0:T(512)S(1)} %log_add_fusion, s32[384]{0:T(512)} %param.7), kind=kOutput, calls=%fused_computation.2 | convolution fusion | flops 3625844736 | bytes 18095104 | tf_op jit(solution)/shard_map/dot_general | solution.py:31
  149.2 8.0 %copy.11 = f32[4608,384]{1,0:T(8,128)} copy(f32[4608,384]{0,1:T(8,128)} %convolution_bitcast_fusion) | data formatting | bytes 14155776
  157.3 0.0 copy-start.3
  157.3 0.0 copy-start.4
  157.3 0.0 reduce-scatter.7.cloned.1.call-update
  157.3 0.2 reduce-scatter.5.cloned.1.call-start
  157.5 0.4 copy-done.3
  158.0 0.0 copy-done.4
  158.0 11.5 %fusion.3 = f32[4608,1024]{1,0:T(8,128)} fusion(bf16[384,4608]{0,1:T(8,128)(2,1)S(1)} %copy-done, f32[4608]{0:T(1024)} %param.5, f32[384]{0:T(512)S(1)} %add_rsqrt_fusion, f32[384,1024]{1,0:T(8,128)} %get-tuple-element.12, s32[1024]{0:T(1024)S(1)} %iota_add_fusion, f32[384]{0:T(512)S(1)} %copy-done.3, s32[384]{0:T(512)S(1)} %copy-done.4), kind=kOutput, calls=%fused_computation.8 | convolution fusion | flops 3632922624 | bytes 24013312 | tf_op jit(solution)/shard_map/dot_general | solution.py:47
  169.5 0.0 copy-start.1
  169.5 0.0 reduce-scatter.5.cloned.1.call-update
  169.5 1.1 copy-done.1
  170.6 0.3 copy.9
  170.9 0.8 dynamic_slice.3
  171.6 93.7 %reduce-scatter.7.cloned.1.call-done = f32[576,384]{1,0:T(8,128)} async-done(((f32[4608,384]{1,0:T(8,128)}), f32[576,384]{1,0:T(8,128)}) %reduce-scatter.7.cloned.1.call-update) | async-done | bytes 884752
  265.3 1.5 copy.12
  266.8 0.4 fusion.7
  267.3 23.4 %psum.22 = f32[384]{0:T(512)S(1)} all-reduce(f32[384]{0:T(512)S(1)} %get-tuple-element.10), channel_id=1, replica_groups=mesh['dp'=32,'tensor'=8] {'tensor'}, use_global_device_ids=true, to_apply=%region_7.0 | all-reduce | flops 384 | bytes 3072 | tf_op jit(solution)/shard_map/psum | solution.py:40
  290.7 0.2 subtract_multiply_fusion
  290.9 1.2 copy.10
  292.2 54.0 %psum.23 = f32[576]{0:T(1024)} all-reduce(f32[576]{0:T(1024)S(1)} %get-tuple-element.9), channel_id=1, replica_groups=mesh['dp'=32,'tensor'=8] {'dp'}, use_global_device_ids=true, to_apply=%region_10.0 | all-reduce | flops 576 | bytes 4608 | tf_op jit(solution)/shard_map/psum | solution.py:45
  346.2 71.0 %reduce-scatter.5.cloned.1.call-done = f32[144,1024]{1,0:T(8,128)} async-done(((f32[4608,1024]{1,0:T(8,128)}), f32[144,1024]{1,0:T(8,128)}) %reduce-scatter.5.cloned.1.call-update) | async-done | bytes 589840 | tf_op jit(solution)/shard_map/reduce_scatter | solution.py:46
  (4 shorter events, 0.0 us)
Async XLA Ops:
  7.2 74.9 %all-gather.2.cloned.1.call-start = ((), (), s32[]{:S(2)}) async-start(), calls=%async_computation.2 | async-start | bytes 3981312 | tf_op jit(solution)/shard_map/all_gather | solution.py:13
  7.9 257.4 %reduce-scatter.7.cloned.1.call-start = ((), (), s32[]{:S(2)}) async-start(), calls=%async_computation.4 | async-start | bytes 7962624
  82.1 3.1 copy-start
  137.6 0.6 copy-start.2
  157.3 0.7 copy-start.3
  157.3 0.7 copy-start.4
  157.3 259.9 %reduce-scatter.5.cloned.1.call-start = ((), (), s32[]{:S(2)}) async-start(), calls=%async_computation.3 | async-start | bytes 19464192 | tf_op jit(solution)/shard_map/reduce_scatter | solution.py:46
  169.5 1.1 copy-start.1
Sparse Core Ops, SparseCore 0:
  10.6 71.4 all-gather.1
  157.4 107.8 reduce-scatter.6
  268.6 148.5 reduce-scatter.4
where the time goes:
time: 424 us
  waiting for transfers between devices  240 us (57%)
  blocking collectives  119 us (28%)
  matrix products  31.3 us (7%)
  local copies, waits for them, and re-layouts  14 us (3%)
  between operations  13.8 us (3%)
  other arithmetic  6.05 us (1%)
    unnamed x4, waiting for transfers between devices  94.4 us
    all_gather x1, waiting for transfers between devices, shards(): gathered = lax.all_gather(hidden_input_state, 'tensor', axis=1, tiled=True)  74.1 us
    reduce_scatter x1, waiting for transfers between devices, shards(): lax.psum_scatter(lax.dot_general(normed, dlogits, (((0,), (0,)), ((), ())...  71 us
    psum x1, blocking collectives, shards(): lax.psum(jnp.sum(normed_gradient * normalized_slice, axis=0), 'dp')  54 us
    psum x1, blocking collectives, shards(): row_inner_sum = lax.psum(partial_inner_sum, 'tensor') / width  23.4 us
    pmax x1, blocking collectives, shards(): row_top = lax.pmax(local_top, 'tensor')  22.2 us
    psum x1, blocking collectives, shards(): row_total = lax.psum(local_total * jnp.exp(local_top - row_top), 'tensor')  19.1 us
    unnamed x14, local copies, waits for them, and re-layouts  13.2 us
  transfers between devices with their start and end apart: 3, of which 3 were waited for; matrix products, arithmetic and copies ran while one was open for 4% of the time, Pallas kernels for 0%

commit v1 on v0

--- a/solution.py
+++ b/solution.py
@@ -6,11 +6,16 @@
 epsilon = 1e-06
 
 
+def gather_over(x, name, along):
+    repeated = jnp.stack([x] * lax.axis_size(name))
+    return jnp.concatenate(lax.all_to_all(repeated, name, 0, 0), axis=along)
+
+
 def shards(hidden_input_state, norm_gain, head_weight, target_ids):
     local_cols = hidden_input_state.shape[1]
     vocab_rows = head_weight.shape[1]
     width = head_weight.shape[0]
-    gathered = lax.all_gather(hidden_input_state, "tensor", axis=1, tiled=True)
+    gathered = gather_over(hidden_input_state, "tensor", 1)
     values = gathered.astype(jnp.float32)
     scaled_rows = lax.rsqrt(jnp.mean(values * values, axis=1, keepdims=True) + epsilon)
     normed = (values * scaled_rows * norm_gain[None, :]).astype(jnp.bfloat16)

time: 424 us -> 403 us (0.950)
  waiting for transfers between devices: 240 us -> 208 us
  starting transfers between devices: 0.3 us -> 7.66 us
  matrix products: 31.3 us -> 26.7 us
    all_gather x1 -> x0, waiting for transfers between devices: 74.1 us -> none  [shards(): gathered = lax.all_gather(hidden_input_state, 'tensor', axis=1, tiled=True)]
    all_to_all x0 -> x1, waiting for transfers between devices: none -> 40.9 us  [gather_over(): return jnp.concatenate(lax.all_to_all(repeated, name, 0, 0), axis=along)]
    all_to_all x0 -> x1, starting transfers between devices: none -> 7.43 us  [gather_over(): return jnp.concatenate(lax.all_to_all(repeated, name, 0, 0), axis=along)]
    unnamed x4 -> x3, waiting for transfers between devices: 94.4 us -> 96.2 us
    unnamed x14 -> x12, local copies, waits for them, and re-layouts: 13.2 us -> 13.7 us
where the time goes in v1:
time: 403 us; the launch traced here: 402 us
  waiting for transfers between devices  208 us (52%)
  blocking collectives  119 us (30%)
  matrix products  26.7 us (7%)
  local copies, waits for them, and re-layouts  17.6 us (4%)
  between operations  14.1 us (3%)
  other arithmetic  8.52 us (2%)
  starting transfers between devices  7.66 us (2%)
    unnamed x3, waiting for transfers between devices  96.2 us
    reduce_scatter x1, waiting for transfers between devices, shards(): lax.psum_scatter(lax.dot_general(normed, dlogits, (((0,), (0,)), ((), ())...  71 us
    psum x1, blocking collectives, shards(): lax.psum(jnp.sum(normed_gradient * normalized_slice, axis=0), 'dp')  54 us
    all_to_all x1, waiting for transfers between devices, gather_over(): return jnp.concatenate(lax.all_to_all(repeated, name, 0, 0), axis=along)  40.9 us
    psum x1, blocking collectives, shards(): row_inner_sum = lax.psum(partial_inner_sum, 'tensor') / width  23.4 us
    pmax x1, blocking collectives, shards(): row_top = lax.pmax(local_top, 'tensor')  22.3 us
    psum x1, blocking collectives, shards(): row_total = lax.psum(local_total * jnp.exp(local_top - row_top), 'tensor')  19.7 us
    unnamed x12, local copies, waits for them, and re-layouts  13.7 us
  transfers between devices with their start and end apart: 3, of which 3 were waited for; matrix products, arithmetic and copies ran while one was open for 4% of the time, Pallas kernels for 0%

profile of v1, /device:TPU:4, one launch (start us, length us, event | category | flops | bytes accessed | tf_op | source)
XLA Modules:
  0.0 402.1 jit_solution(9048101862160308798)
XLA Ops:
  7.2 3.1 stack.2
  10.2 7.4 %all-to-all-start = ((bf16[8,384,576]{1,2,0:T(8,128)(2,1)}), bf16[8,384,576]{1,2,0:T(8,128)(2,1)S(1)}, u32[]{:S(2)}, u32[]{:S(2)}) async-start(bf16[8,384,576]{1,2,0:T(8,128)(2,1)} %stack.2), calls=%async_computation | async-start | bytes 7077888 | tf_op jit(solution)/shard_map/all_to_all | solution.py:11
  17.7 0.0 reduce-scatter.7.cloned.1.call-start
  17.7 40.9 %all-to-all-done = bf16[8,384,576]{1,2,0:T(8,128)(2,1)S(1)} async-done(((bf16[8,384,576]{1,2,0:T(8,128)(2,1)}), bf16[8,384,576]{1,2,0:T(8,128)(2,1)S(1)}, u32[]{:S(2)}, u32[]{:S(2)}) %all-to-all-start) | async-done | bytes 3538976 | tf_op jit(solution)/shard_map/all_to_all | solution.py:11
  58.6 0.0 copy-start
  58.6 0.0 copy-start.1
  58.6 0.8 multiply_reduce_fusion
  59.4 1.0 copy-done
  60.4 3.9 fusion.1
  64.4 0.3 copy-done.1
  64.7 5.0 %fusion.4 = (f32[384]{0:T(512)S(1)}, f32[384,1024]{1,0:T(8,128)}) fusion(bf16[384,4608]{0,1:T(8,128)(2,1)S(1)} %fusion.1, bf16[4608,1024]{1,0:T(8,128)(2,1)S(1)} %copy-done.1), kind=kOutput, calls=%fused_computation.19 | convolution fusion | flops 3624271360 | bytes 14550528 | tf_op jit(solution)/shard_map/dot_general | solution.py:22
  69.7 22.3 %pmax.7 = f32[384]{0:T(512)S(1)} all-reduce(f32[384]{0:T(512)S(1)} %get-tuple-element.14), channel_id=1, replica_groups=mesh['dp'=32,'tensor'=8] {'tensor'}, use_global_device_ids=true, to_apply=%region_2.0 | all-reduce | flops 384 | bytes 3072 | tf_op jit(solution)/shard_map/pmax | solution.py:25
  92.0 1.8 exponential_reduce_fusion
  93.8 0.6 exponential_multiply_fusion
  94.4 19.7 %psum.21 = f32[384]{0:T(512)} all-reduce(f32[384]{0:T(512)} %exponential_multiply_fusion), channel_id=1, replica_groups=mesh['dp'=32,'tensor'=8] {'tensor'}, use_global_device_ids=true, to_apply=%region_4.0 | all-reduce | flops 384 | bytes 3072 | tf_op jit(solution)/shard_map/psum | solution.py:26
  114.0 0.7 log_add_fusion
  114.7 11.1 %convolution_bitcast_fusion = f32[4608,384]{0,1:T(8,128)} fusion(bf16[4608,1024]{1,0:T(8,128)(2,1)} %param.6, f32[384,1024]{1,0:T(8,128)} %get-tuple-element.15, s32[1024]{0:T(1024)S(1)} %iota_add_fusion, f32[384]{0:T(512)S(1)} %log_add_fusion, s32[384]{0:T(512)} %param.7), kind=kOutput, calls=%fused_computation | convolution fusion | flops 3625844736 | bytes 18095104 | tf_op jit(solution)/shard_map/dot_general | solution.py:36
  125.8 8.0 %copy.14 = f32[4608,384]{1,0:T(8,128)} copy(f32[4608,384]{0,1:T(8,128)} %convolution_bitcast_fusion) | data formatting | bytes 14155776
  133.8 0.0 copy-start.3
  133.8 0.0 reduce-scatter.7.cloned.1.call-update
  133.8 0.2 reduce-scatter.5.cloned.1.call-start
  134.1 0.4 copy-done.3
  134.5 10.7 %fusion.3 = f32[4608,1024]{1,0:T(8,128)} fusion(bf16[384,4608]{0,1:T(8,128)(2,1)S(1)} %fusion.1, f32[384,1024]{1,0:T(8,128)} %get-tuple-element.15, s32[1024]{0:T(1024)S(1)} %iota_add_fusion, f32[384]{0:T(512)S(1)} %log_add_fusion, s32[384]{0:T(512)S(1)} %copy-done.3), kind=kOutput, calls=%fused_computation.18 | convolution fusion | flops 3625844736 | bytes 23993344 | tf_op jit(solution)/shard_map/dot_general | solution.py:52
  145.2 0.0 copy-start.2
  145.2 0.0 reduce-scatter.5.cloned.1.call-update
  145.2 1.0 copy-done.2
  146.2 0.3 copy.12
  146.4 0.8 dynamic_slice.3
  147.2 96.1 %reduce-scatter.7.cloned.1.call-done = f32[576,384]{1,0:T(8,128)} async-done(((f32[4608,384]{1,0:T(8,128)}), f32[576,384]{1,0:T(8,128)}) %reduce-scatter.7.cloned.1.call-update) | async-done | bytes 884752
  243.4 1.5 copy.15
  244.9 0.4 fusion.2
  245.3 23.4 %psum.22 = f32[384]{0:T(512)S(1)} all-reduce(f32[384]{0:T(512)S(1)} %get-tuple-element.13), channel_id=1, replica_groups=mesh['dp'=32,'tensor'=8] {'tensor'}, use_global_device_ids=true, to_apply=%region_7.0 | all-reduce | flops 384 | bytes 3072 | tf_op jit(solution)/shard_map/psum | solution.py:45
  268.7 0.2 subtract_multiply_fusion
  269.0 1.2 copy.13
  270.2 54.0 %psum.23 = f32[576]{0:T(1024)} all-reduce(f32[576]{0:T(1024)S(1)} %get-tuple-element.12), channel_id=1, replica_groups=mesh['dp'=32,'tensor'=8] {'dp'}, use_global_device_ids=true, to_apply=%region_10.0 | all-reduce | flops 576 | bytes 4608 | tf_op jit(solution)/shard_map/psum | solution.py:50
  324.2 71.0 %reduce-scatter.5.cloned.1.call-done = f32[144,1024]{1,0:T(8,128)} async-done(((f32[4608,1024]{1,0:T(8,128)}), f32[144,1024]{1,0:T(8,128)}) %reduce-scatter.5.cloned.1.call-update) | async-done | bytes 589840 | tf_op jit(solution)/shard_map/reduce_scatter | solution.py:51
  (3 shorter events, 0.0 us)
Async XLA Ops:
  10.2 48.4 %all-to-all-start = ((bf16[8,384,576]{1,2,0:T(8,128)(2,1)}), bf16[8,384,576]{1,2,0:T(8,128)(2,1)S(1)}, u32[]{:S(2)}, u32[]{:S(2)}) async-start(bf16[8,384,576]{1,2,0:T(8,128)(2,1)} %stack.2), calls=%async_computation | async-start | bytes 7077888 | tf_op jit(solution)/shard_map/all_to_all | solution.py:11
  17.7 225.7 %reduce-scatter.7.cloned.1.call-start = ((), (), s32[]{:S(2)}) async-start(), calls=%async_computation.4 | async-start | bytes 7962624
  58.6 1.8 copy-start
  58.6 6.1 %copy-start.1 = (bf16[4608,1024]{1,0:T(8,128)(2,1)S(1)}, bf16[4608,1024]{1,0:T(8,128)(2,1)}, u32[]{:S(2)}) copy-start(bf16[4608,1024]{1,0:T(8,128)(2,1)} %param.6) | copy-start | bytes 28311556
  133.8 0.7 copy-start.3
  133.8 261.4 %reduce-scatter.5.cloned.1.call-start = ((), (), s32[]{:S(2)}) async-start(), calls=%async_computation.3 | async-start | bytes 19464192 | tf_op jit(solution)/shard_map/reduce_scatter | solution.py:51
  145.2 1.0 copy-start.2
Sparse Core Ops, SparseCore 0:
  134.0 109.3 reduce-scatter.6
  246.7 148.5 reduce-scatter.4
